TPU v7x, 32 devices: a whole 2x2x4 slice. The times are simulated.
32 devices in a mesh: groups: 2 (over x), seq: 8 (over z, y), chan: 2 (over core).
Axes of the slice: x: 2, y: 2, z: 4, core: 2. Of those that a mesh axis runs over, the one named last changes fastest.
Arguments:
- cached_input: bfloat16 [2048, 4096], P(('groups', 'seq'), 'chan'), parts along dimension 0, may hold values from -6 to 6
- cached_gate: bfloat16 [2048, 4096], P(('groups', 'seq'), 'chan'), parts along dimension 0, may hold values from -6 to 6
- out_grad: bfloat16 [2048, 4096], P(('groups', 'seq'), 'chan'), parts along dimension 0, may hold values from -1.75 to 1.75
- filter_taps: bfloat16 [1024, 32], P('seq', 'chan'), may hold values from -6 to 6
- skip_gain: float32 [4096], P('chan'), may hold values from -1 to 1
Outputs:
- input_grad: bfloat16 [2048, 4096], P(('groups', 'seq'), 'chan'), parts along dimension 0
- filter_grad: float32 [2048, 32], P(('groups', 'seq'), 'chan'), parts along dimension 0
There are 2 independent parts, one for each index of `groups`. A program takes and returns all parts, laid end to end along the dimension named above; an argument that names none is the same for every part. Nothing has to cross between parts.
All inputs are finite; a program needn't handle non-finite values.
Results may differ from a plain program's by a relative error of at most 0.005.
Values may be sent and summed in bfloat16 or wider, within the bound.
No kernel may reach another device: no remote copies, remote signals or barrier semaphores. Data moves between devices by JAX's collectives and lax.ppermute only.
A program may use at most 64 MiB of HBM per device.

v0:
```python
import math
import jax
import numpy as np
import jax.numpy as jnp
from jax import lax
from jax.sharding import PartitionSpec as P

lag_group = 4


def toeplitz_blocks(windows, block_rows):
    flipped = windows[..., ::-1]
    tiled = jnp.tile(flipped, (1, 1, block_rows))
    trimmed = tiled[..., : block_rows * (2 * block_rows - 1)]
    shaped = trimmed.reshape(windows.shape[0], windows.shape[1], block_rows, 2 * block_rows - 1)
    return shaped[..., block_rows - 1 : 2 * block_rows - 1]


def diagonal_sums(products, block_rows):
    flipped = products[..., ::-1]
    padded = jnp.pad(flipped, ((0, 0), (0, 0), (0, 0), (0, block_rows)))
    flattened = padded.reshape(products.shape[0], products.shape[1], 2 * block_rows * block_rows)
    trimmed = flattened[..., : block_rows * (2 * block_rows - 1)]
    shaped = trimmed.reshape(products.shape[0], products.shape[1], block_rows, 2 * block_rows - 1)
    diag_sums = jnp.sum(shaped, axis=2)
    return jnp.pad(diag_sums, ((0, 0), (0, 0), (1, 0)))


def fold_windows(window_grads, block_rows):
    front_half = jnp.pad(window_grads[..., :block_rows], ((0, 1), (0, 0), (0, 0)))
    back_half = jnp.pad(window_grads[..., block_rows:], ((1, 0), (0, 0), (0, 0)))
    joined = front_half + back_half
    return jnp.transpose(joined, (1, 0, 2)).reshape(window_grads.shape[1], -1)


def lag_table(taps_all, block_rows):
    return jnp.pad(jnp.transpose(taps_all), ((0, 0), (block_rows, lag_group * block_rows)))


def lag_sweep(
    blocks, base_block, block_count, sources, tap_table, block_rows, trip_count, seq_count
):
    filters = sources.shape[2]
    group_width = sources.shape[3]

    def advance(lag_step, state_pair):
        input_acc, lag_acc = state_pair
        lag_start = lag_step * lag_group
        stacked = jnp.stack(
            [
                lax.dynamic_slice_in_dim(blocks, base_block + lag_start + offset, block_count, 0)
                for offset in range(lag_group)
            ],
            axis=1,
        )
        lag_span = lax.dynamic_slice_in_dim(
            tap_table, lag_start * block_rows, (lag_group + 1) * block_rows, 1
        )
        windows = jnp.stack(
            [
                lag_span[:, offset * block_rows : (offset + 2) * block_rows]
                for offset in range(lag_group)
            ],
            axis=0,
        )
        toeplitz = toeplitz_blocks(windows, block_rows)
        input_acc = input_acc + jnp.einsum(
            "kfts,iktfg->isfg", toeplitz, stacked, preferred_element_type=jnp.float32
        )
        products = jnp.einsum(
            "iktfg,isfg->kfts", stacked, sources, preferred_element_type=jnp.float32
        )
        folded = fold_windows(diagonal_sums(products, block_rows), block_rows)
        previous = lax.dynamic_slice_in_dim(
            lag_acc, lag_start * block_rows, (lag_group + 1) * block_rows, 1
        )
        lag_acc = lax.dynamic_update_slice_in_dim(
            lag_acc, previous + folded, lag_start * block_rows, 1
        )
        return (input_acc, lag_acc)

    initial = (
        jnp.zeros((block_count, block_rows, filters, group_width), jnp.float32),
        jnp.zeros((filters, (seq_count + 1 + lag_group) * block_rows), jnp.float32),
    )
    return lax.fori_loop(0, trip_count, advance, initial)


def per_device(cached_input, cached_gate, out_grad, filter_taps, skip_gain):
    block_rows = cached_input.shape[0]
    chan_width = cached_input.shape[1]
    filters = filter_taps.shape[1]
    group_width = chan_width // filters
    seq_count = lax.axis_size("seq")
    seq_index = lax.axis_index("seq")
    length = block_rows * seq_count
    taps_scale = 1.0 / math.sqrt(length)
    gated_grad = (out_grad.astype(jnp.float32) * cached_gate.astype(jnp.float32)).astype(
        jnp.bfloat16
    )
    stretch_width = chan_width // seq_count
    stretch_filters = max(1, stretch_width // group_width)
    stretch_group = stretch_width // stretch_filters
    first_filter = seq_index * stretch_width // group_width
    tap_columns = np.array(
        [
            target * stretch_width // group_width + offset
            for target in range(seq_count)
            for offset in range(stretch_filters)
        ]
    )
    routed_taps = filter_taps[:, tap_columns].reshape(block_rows, seq_count, stretch_filters)
    packed = jnp.concatenate(
        [
            gated_grad.reshape(block_rows, seq_count, stretch_width),
            cached_input.reshape(block_rows, seq_count, stretch_width),
            routed_taps,
        ],
        axis=2,
    )
    moved = lax.all_to_all(packed, "seq", split_axis=1, concat_axis=0, tiled=True)
    moved = moved.reshape(length, 2 * stretch_width + stretch_filters)
    moved_grad = moved[:, :stretch_width]
    moved_input = moved[:, stretch_width : 2 * stretch_width]
    stretch_taps = moved[:, 2 * stretch_width :]
    shaped_grad = moved_grad.reshape(seq_count, block_rows, stretch_filters, stretch_group)
    blocks = jnp.pad(shaped_grad, ((0, seq_count - 1 + lag_group), (0, 0), (0, 0), (0, 0)))
    sources = moved_input.reshape(seq_count, block_rows, stretch_filters, stretch_group)
    trip_count = (seq_count + lag_group - 1) // lag_group
    input_acc, lag_acc = lag_sweep(
        blocks,
        0,
        seq_count,
        sources,
        lag_table(stretch_taps, block_rows),
        block_rows,
        trip_count,
        seq_count,
    )
    stretch_gain = lax.dynamic_slice_in_dim(skip_gain, seq_index * stretch_width, stretch_width, 0)
    conv_grad = input_acc.reshape(length, stretch_width) * taps_scale
    local_grad = (conv_grad + stretch_gain[None, :] * moved_grad.astype(jnp.float32)).astype(
        jnp.bfloat16
    )
    input_grad = lax.all_to_all(local_grad, "seq", split_axis=0, concat_axis=1, tiled=True)
    stretch_term = jnp.transpose(lag_acc[:, block_rows : block_rows + length]) * taps_scale
    lag_parts = lax.all_to_all(
        stretch_term.reshape(seq_count, block_rows, stretch_filters),
        "seq",
        split_axis=0,
        concat_axis=0,
        tiled=True,
    )
    sharers = seq_count * stretch_filters // filters
    filter_grad = (
        jnp.transpose(lag_parts, (1, 0, 2)).reshape(block_rows, filters, sharers).sum(axis=2)
    )
    return (input_grad, filter_grad)


def solution(mesh):
    return jax.shard_map(
        per_device,
        mesh=mesh,
        in_specs=(
            P(("groups", "seq"), "chan"),
            P(("groups", "seq"), "chan"),
            P(("groups", "seq"), "chan"),
            P("seq", "chan"),
            P("chan"),
        ),
        out_specs=(P(("groups", "seq"), "chan"), P(("groups", "seq"), "chan")),
        check_vma=False,
    )
```

profile of v0, /device:TPU:0, one launch (start us, length us, event | category | flops | bytes accessed | tf_op | source)
XLA Modules:
  0.0 98.7 jit_solution(5453652676311803673)
XLA Ops:
  0.7 1.4 %copy.32 = bf16[128,2048]{0,1:T(8,128)(2,1)S(1)} copy(bf16[128,2048]{1,0:T(8,128)(2,1)} %param.9) | data formatting | bytes 1048576 | tf_op args[0]
  3.1 1.1 %pad_maximum_fusion.4 = bf16[128,8,514]{0,2,1:T(8,128)(2,1)} fusion(bf16[128,8,2]{0,2,1:T(2,128)(2,1)S(1)} %bitcast.138, bf16[128,8,256]{0,2,1:T(8,128)(2,1)S(1)} %bitcast.136, bf16[128,8,256]{0,2,1:T(8,128)(2,1)S(1)} %bitcast.137), kind=kLoop, calls=%fused_computation.25 | loop fusion | flops 3158016 | bytes 2105344 | tf_op jit(solution)/shard_map/concatenate | solution.py:113
  4.2 7.3 %all-to-all-start = ((bf16[128,8,514]{0,2,1:T(8,128)(2,1)}), bf16[128,8,514]{0,2,1:T(8,128)(2,1)S(1)}, u32[]{:S(2)}, u32[]{:S(2)}) async-start(bf16[128,8,514]{0,2,1:T(8,128)(2,1)} %pad_maximum_fusion.4), calls=%async_computation | async-start | bytes 2129920 | tf_op jit(solution)/shard_map/all_to_all | solution.py:121
  11.4 0.8 dynamic_slice.63
  12.2 25.4 %all-to-all-done = bf16[128,8,514]{0,2,1:T(8,128)(2,1)S(1)} async-done(((bf16[128,8,514]{0,2,1:T(8,128)(2,1)}), bf16[128,8,514]{0,2,1:T(8,128)(2,1)S(1)}, u32[]{:S(2)}, u32[]{:S(2)}) %all-to-all-start) | async-done | bytes 1052704 | tf_op jit(solution)/shard_map/all_to_all | solution.py:121
  38.3 0.8 copy-done.3
  39.5 1.1 %copy.35 = bf16[8,128,2,128]{3,1,0,2:T(8,128)(2,1)} copy(bf16[8,128,2,128]{1,0,3,2:T(8,128)(2,1)S(1)} %bitcast.135) | data formatting | bytes 1048576
  40.6 26.8 %while.18 = (s32[]{:T(128)}, f32[8,128,2,128]{1,3,0,2:T(8,128)}, f32[2,1664]{1,0:T(2,128)S(1)}, bf16[19,128,2,128]{1,3,0,2:T(8,128)(2,1)S(1)}, bf16[2,1664]{1,0:...) while((s32[]{:T(128)}, f32[8,128,2,128]{1,3,0,2:T(8,128)}, ...), condition=%wide.region_2.3_spmd.clone, body=%wide.region_0.2_spmd.clone.sunk | while | flops 543954432 | bytes 31783416 | solution.py:86
  40.6 1.2 %dynamic-slice_bitcast_fusion.5 = (bf16[8,1,128,2,128]{2,4,1,0,3:T(8,128)(2,1)S(1)}, bf16[8,1,128,2,128]{2,4,1,0,3:T(8,128)(2,1)S(1)}, bf16[8,1,128,2,128]{2,4,1,0,3:T(8,128)(2,1)}, bf16[8,1,128,2,128]{2,4,1,0,3:T(8,128)(2,1)}) fusion(bf16[19,128,2,128]{1,3,0,2:T(8,128)(2,1)S(1)} %get-tuple-element.324, s32[]{:T(128)S(6)} %select_n.70, ...), kind=kLoop, calls=%fused_computation.9.clone.1 | loop fusion | bytes 4194320 | tf_op jit(solution)/shard_map/while/body/eval_jaxpr/stack | solution.py:49
  42.6 1.6 %reshape.107 = bf16[4,2,128,255]{3,2,1,0:T(8,128)(2,1)S(1)} reshape(bf16[4,2,32640]{2,1,0:T(2,128)(2,1)S(1)} %slice.144) | data formatting | bytes 1044480 | tf_op jit(solution)/shard_map/while/body/eval_jaxpr/reshape | solution.py:15
  44.2 3.1 %fusion.21 = f32[8,128,2,128]{1,3,0,2:T(8,128)} fusion(f32[8,128,2,128]{1,3,0,2:T(8,128)} %get-tuple-element.301, pred[]{:T(512)S(6)} %compare.9, bf16[8,1,128,2,128]{2,4,1,0,3:T(8,128)(2,1)S(1)} %get-tuple-element.269, bf16[8,1,128,2,128]{2,4,1,0,3:T(8,128)(2,1)} %get-tuple-element.270, bf16[8,1,128,2,128]{2,4,1,0,3:T(8,128)(2,1)} %get-tuple-element.271, ...), kind=kOutput, calls=%fused_computation.3.clone.1 | convolution fusion | flops 272105472 | bytes 4456449 | tf_op jit(solution)/shard_map/while/body/eval_jaxpr/kfts,iktfg->isfg/dot_general | solution.py:67
  47.3 1.1 %convolution_bitcast_fusion.3 = f32[4,2,128,128]{3,2,0,1:T(8,128)S(1)} fusion(bf16[8,128,2,128]{3,1,0,2:T(8,128)(2,1)S(1)} %copy-done.6, bf16[8,1,128,2,128]{2,4,1,0,3:T(8,128)(2,1)S(1)} %get-tuple-element.269, bf16[8,1,128,2,128]{2,4,1,0,3:T(8,128)(2,1)S(1)} %copy-done.1, bf16[8,1,128,2,128]{2,4,1,0,3:T(8,128)(2,1)S(1)} %copy-done.2, ...), kind=kOutput, calls=%fused_computation.4.clone.1 | convolution fusion | flops 271581184 | bytes 3145728 | tf_op jit(solution)/shard_map/while/body/eval_jaxpr/iktfg,isfg->kfts/dot_general | solution.py:70
  48.4 0.7 rev.25
  49.8 1.0 %slice.145 = f32[4,2,32640]{2,0,1:T(4,128)} slice(f32[4,2,32768]{2,0,1:T(4,128)S(1)} %reshape.108), slice={[0:4], [0:2], [0:32640]} | slice | bytes 2088960 | tf_op jit(solution)/shard_map/while/body/eval_jaxpr/slice | solution.py:23
  50.8 2.8 %reshape.109 = f32[4,2,128,255]{3,2,0,1:T(8,128)S(1)} reshape(f32[4,2,32640]{2,0,1:T(4,128)} %slice.145) | data formatting | bytes 2088960 | tf_op jit(solution)/shard_map/while/body/eval_jaxpr/reshape | solution.py:24
  53.9 1.2 %dynamic-slice_bitcast_fusion.5 = (bf16[8,1,128,2,128]{2,4,1,0,3:T(8,128)(2,1)S(1)}, bf16[8,1,128,2,128]{2,4,1,0,3:T(8,128)(2,1)S(1)}, bf16[8,1,128,2,128]{2,4,1,0,3:T(8,128)(2,1)}, bf16[8,1,128,2,128]{2,4,1,0,3:T(8,128)(2,1)}) fusion(bf16[19,128,2,128]{1,3,0,2:T(8,128)(2,1)S(1)} %get-tuple-element.324, s32[]{:T(128)S(6)} %select_n.70, ...), kind=kLoop, calls=%fused_computation.9.clone.1 | loop fusion | bytes 4194320 | tf_op jit(solution)/shard_map/while/body/eval_jaxpr/stack | solution.py:49
  55.8 1.6 %reshape.107 = bf16[4,2,128,255]{3,2,1,0:T(8,128)(2,1)S(1)} reshape(bf16[4,2,32640]{2,1,0:T(2,128)(2,1)S(1)} %slice.144) | data formatting | bytes 1044480 | tf_op jit(solution)/shard_map/while/body/eval_jaxpr/reshape | solution.py:15
  57.4 3.5 %fusion.21 = f32[8,128,2,128]{1,3,0,2:T(8,128)} fusion(f32[8,128,2,128]{1,3,0,2:T(8,128)} %get-tuple-element.301, pred[]{:T(512)S(6)} %compare.9, bf16[8,1,128,2,128]{2,4,1,0,3:T(8,128)(2,1)S(1)} %get-tuple-element.269, bf16[8,1,128,2,128]{2,4,1,0,3:T(8,128)(2,1)} %get-tuple-element.270, bf16[8,1,128,2,128]{2,4,1,0,3:T(8,128)(2,1)} %get-tuple-element.271, ...), kind=kOutput, calls=%fused_computation.3.clone.1 | convolution fusion | flops 272105472 | bytes 4456449 | tf_op jit(solution)/shard_map/while/body/eval_jaxpr/kfts,iktfg->isfg/dot_general | solution.py:67
  60.9 1.1 %convolution_bitcast_fusion.3 = f32[4,2,128,128]{3,2,0,1:T(8,128)S(1)} fusion(bf16[8,128,2,128]{3,1,0,2:T(8,128)(2,1)S(1)} %copy-done.6, bf16[8,1,128,2,128]{2,4,1,0,3:T(8,128)(2,1)S(1)} %get-tuple-element.269, bf16[8,1,128,2,128]{2,4,1,0,3:T(8,128)(2,1)S(1)} %copy-done.1, bf16[8,1,128,2,128]{2,4,1,0,3:T(8,128)(2,1)S(1)} %copy-done.2, ...), kind=kOutput, calls=%fused_computation.4.clone.1 | convolution fusion | flops 271581184 | bytes 3145728 | tf_op jit(solution)/shard_map/while/body/eval_jaxpr/iktfg,isfg->kfts/dot_general | solution.py:70
  62.0 0.7 rev.25
  63.4 1.0 %slice.145 = f32[4,2,32640]{2,0,1:T(4,128)} slice(f32[4,2,32768]{2,0,1:T(4,128)S(1)} %reshape.108), slice={[0:4], [0:2], [0:32640]} | slice | bytes 2088960 | tf_op jit(solution)/shard_map/while/body/eval_jaxpr/slice | solution.py:23
  64.4 2.8 %reshape.109 = f32[4,2,128,255]{3,2,0,1:T(8,128)S(1)} reshape(f32[4,2,32640]{2,0,1:T(4,128)} %slice.145) | data formatting | bytes 2088960 | tf_op jit(solution)/shard_map/while/body/eval_jaxpr/reshape | solution.py:24
  67.5 1.3 %broadcast_multiply_fusion = f32[8,128,2,128]{1,3,0,2:T(8,128)S(1)} fusion(f32[8,128,2,128]{1,3,0,2:T(8,128)} %get-tuple-element.161), kind=kLoop, calls=%fused_computation.33 | loop fusion | flops 262144 | bytes 2097152 | tf_op jit(solution)/shard_map/mul | solution.py:141
  68.8 0.6 copy.36
  69.4 0.6 multiply_bitcast_fusion
  70.0 3.6 %all-to-all-start.2 = ((f32[8,128,2]{1,2,0:T(2,128)}), f32[8,128,2]{1,2,0:T(2,128)S(1)}, u32[]{:S(2)}, u32[]{:S(2)}) async-start(f32[8,128,2]{1,2,0:T(2,128)} %multiply_bitcast_fusion), calls=%async_computation.2 | async-start | bytes 16384 | tf_op jit(solution)/shard_map/all_to_all | solution.py:147
  73.6 2.1 %copy_bitcast_fusion.3 = bf16[8,128,256]{1,2,0:T(8,128)(2,1)} fusion(f32[32,8,8,128]{3,2,1,0:T(8,128)S(1)} %bitcast.132, f32[256]{0:T(256)S(1)} %dynamic_slice.63, bf16[1024,514]{0,1:T(8,128)(2,1)} %bitcast.128), kind=kLoop, calls=%fused_computation.31 | loop fusion | flops 1048576 | bytes 2098176 | tf_op jit(solution)/shard_map/all_to_all | solution.py:145
  75.7 4.4 %all-to-all-done.2 = f32[8,128,2]{1,2,0:T(2,128)S(1)} async-done(((f32[8,128,2]{1,2,0:T(2,128)}), f32[8,128,2]{1,2,0:T(2,128)S(1)}, u32[]{:S(2)}, u32[]{:S(2)}) %all-to-all-start.2) | async-done | bytes 8224 | tf_op jit(solution)/shard_map/all_to_all | solution.py:147
  80.1 3.5 %all-to-all-start.1 = ((bf16[8,128,256]{1,2,0:T(8,128)(2,1)}), bf16[8,128,256]{1,2,0:T(8,128)(2,1)S(1)}, u32[]{:S(2)}, u32[]{:S(2)}) async-start(bf16[8,128,256]{1,2,0:T(8,128)(2,1)} %copy_bitcast_fusion.3), calls=%async_computation.1 | async-start | bytes 1048576 | tf_op jit(solution)/shard_map/all_to_all | solution.py:145
  83.6 13.4 %all-to-all-done.1 = bf16[8,128,256]{1,2,0:T(8,128)(2,1)S(1)} async-done(((bf16[8,128,256]{1,2,0:T(8,128)(2,1)}), bf16[8,128,256]{1,2,0:T(8,128)(2,1)S(1)}, u32[]{:S(2)}, u32[]{:S(2)}) %all-to-all-start.1) | async-done | bytes 524320 | tf_op jit(solution)/shard_map/all_to_all | solution.py:145
  97.1 1.0 %copy.39 = bf16[128,2048]{1,0:T(8,128)(2,1)} copy(bf16[128,2048]{0,1:T(8,128)(2,1)S(1)} %bitcast.133) | data formatting | bytes 1048576
  98.1 0.6 copy.79
  (60 shorter events, 5.2 us)
Async XLA Ops:
  0.6 1.9 %copy-start = (bf16[128,16]{0,1:T(8,128)(2,1)S(1)}, bf16[128,16]{0,1:T(8,128)(2,1)}, u32[]{:S(2)}) copy-start(bf16[128,16]{0,1:T(8,128)(2,1)} %param.12) | copy-start | bytes 12292
  0.6 1.4 %copy-start.4 = (bf16[128,2048]{1,0:T(8,128)(2,1)S(1)}, bf16[128,2048]{1,0:T(8,128)(2,1)}, u32[]{:S(2)}) copy-start(bf16[128,2048]{1,0:T(8,128)(2,1)} %param.10) | copy-start | bytes 1572868
  0.7 1.4 %copy-start.5 = (bf16[128,2048]{1,0:T(8,128)(2,1)S(1)}, bf16[128,2048]{1,0:T(8,128)(2,1)}, u32[]{:S(2)}) copy-start(bf16[128,2048]{1,0:T(8,128)(2,1)} %param.11) | copy-start | bytes 1572868
  4.2 33.4 %all-to-all-start = ((bf16[128,8,514]{0,2,1:T(8,128)(2,1)}), bf16[128,8,514]{0,2,1:T(8,128)(2,1)S(1)}, u32[]{:S(2)}, u32[]{:S(2)}) async-start(bf16[128,8,514]{0,2,1:T(8,128)(2,1)} %pad_maximum_fusion.4), calls=%async_computation | async-start | bytes 2129920 | tf_op jit(solution)/shard_map/all_to_all | solution.py:121
  38.1 1.0 copy-start.3
  44.1 3.2 %copy-start.1 = (bf16[8,1,128,2,128]{2,4,1,0,3:T(8,128)(2,1)S(1)}, bf16[8,1,128,2,128]{2,4,1,0,3:T(8,128)(2,1)}, u32[]{:S(2)}) copy-start(bf16[8,1,128,2,128]{2,4,1,0,3:T(8,128)(2,1)} %get-tuple-element.270) | copy-start | bytes 1572868 | tf_op jit(solution)/shard_map/while
  44.1 3.2 %copy-start.2 = (bf16[8,1,128,2,128]{2,4,1,0,3:T(8,128)(2,1)S(1)}, bf16[8,1,128,2,128]{2,4,1,0,3:T(8,128)(2,1)}, u32[]{:S(2)}) copy-start(bf16[8,1,128,2,128]{2,4,1,0,3:T(8,128)(2,1)} %get-tuple-element.271) | copy-start | bytes 1572868 | tf_op jit(solution)/shard_map/while
  44.2 3.1 %copy-start.6 = (bf16[8,128,2,128]{3,1,0,2:T(8,128)(2,1)S(1)}, bf16[8,128,2,128]{3,1,0,2:T(8,128)(2,1)}, u32[]{:S(2)}) copy-start(bf16[8,128,2,128]{3,1,0,2:T(8,128)(2,1)} %get-tuple-element.326) | copy-start | bytes 1572868 | tf_op jit(solution)/shard_map/while
  57.4 3.5 %copy-start.1 = (bf16[8,1,128,2,128]{2,4,1,0,3:T(8,128)(2,1)S(1)}, bf16[8,1,128,2,128]{2,4,1,0,3:T(8,128)(2,1)}, u32[]{:S(2)}) copy-start(bf16[8,1,128,2,128]{2,4,1,0,3:T(8,128)(2,1)} %get-tuple-element.270) | copy-start | bytes 1572868 | tf_op jit(solution)/shard_map/while
  57.4 3.5 %copy-start.2 = (bf16[8,1,128,2,128]{2,4,1,0,3:T(8,128)(2,1)S(1)}, bf16[8,1,128,2,128]{2,4,1,0,3:T(8,128)(2,1)}, u32[]{:S(2)}) copy-start(bf16[8,1,128,2,128]{2,4,1,0,3:T(8,128)(2,1)} %get-tuple-element.271) | copy-start | bytes 1572868 | tf_op jit(solution)/shard_map/while
  57.4 3.5 %copy-start.6 = (bf16[8,128,2,128]{3,1,0,2:T(8,128)(2,1)S(1)}, bf16[8,128,2,128]{3,1,0,2:T(8,128)(2,1)}, u32[]{:S(2)}) copy-start(bf16[8,128,2,128]{3,1,0,2:T(8,128)(2,1)} %get-tuple-element.326) | copy-start | bytes 1572868 | tf_op jit(solution)/shard_map/while
  70.0 10.1 %all-to-all-start.2 = ((f32[8,128,2]{1,2,0:T(2,128)}), f32[8,128,2]{1,2,0:T(2,128)S(1)}, u32[]{:S(2)}, u32[]{:S(2)}) async-start(f32[8,128,2]{1,2,0:T(2,128)} %multiply_bitcast_fusion), calls=%async_computation.2 | async-start | bytes 16384 | tf_op jit(solution)/shard_map/all_to_all | solution.py:147
  80.1 16.9 %all-to-all-start.1 = ((bf16[8,128,256]{1,2,0:T(8,128)(2,1)}), bf16[8,128,256]{1,2,0:T(8,128)(2,1)S(1)}, u32[]{:S(2)}, u32[]{:S(2)}) async-start(bf16[8,128,256]{1,2,0:T(8,128)(2,1)} %copy_bitcast_fusion.3), calls=%async_computation.1 | async-start | bytes 1048576 | tf_op jit(solution)/shard_map/all_to_all | solution.py:145
where the time goes:
time: 99.2 us; the launch traced here: 98.7 us
  waiting for transfers between devices  43.2 us (44%)
  local copies, waits for them, and re-layouts  25.7 us (26%)
  starting transfers between devices  14.4 us (15%)
  matrix products  8.83 us (9%)
  other arithmetic  5.49 us (6%)
    all_to_all x1, waiting for transfers between devices, per_device(): lax.all_to_all(packed, 'seq', split_axis=1, concat_axis=0, tiled=True)  25.4 us
    all_to_all x1, waiting for transfers between devices, per_device(): lax.all_to_all(local_grad, 'seq', split_axis=0, concat_axis=1, tiled=True)  13.4 us
    all_to_all x1, starting transfers between devices, per_device(): lax.all_to_all(packed, 'seq', split_axis=1, concat_axis=0, tiled=True)  7.28 us
    dot_general x2, matrix products, advance(): jnp.einsum('kfts,iktfg->isfg', toeplitz, stacked, preferred_element_type=...  6.6 us
    reshape x2, local copies, waits for them, and re-layouts, diagonal_sums(): trimmed.reshape(products.shape[0], products.shape[1], block_rows, 2 * blo...  5.62 us
    unnamed x17, local copies, waits for them, and re-layouts  5.54 us
    all_to_all x1, waiting for transfers between devices, per_device(): lax.all_to_all(stretch_term.reshape(seq_count, block_rows, stretch_filter...  4.37 us
    all_to_all x1, starting transfers between devices, per_device(): lax.all_to_all(stretch_term.reshape(seq_count, block_rows, stretch_filter...  3.59 us
  transfers between devices with their start and end apart: 3, of which 3 were waited for; matrix products, arithmetic and copies ran while one was open for 3% of the time, Pallas kernels for 0%

commit v1 on v0

--- a/solution.py
+++ b/solution.py
@@ -142,7 +142,10 @@
     local_grad = (conv_grad + stretch_gain[None, :] * moved_grad.astype(jnp.float32)).astype(
         jnp.bfloat16
     )
-    input_grad = lax.all_to_all(local_grad, "seq", split_axis=0, concat_axis=1, tiled=True)
+    input_grad = jnp.concatenate(
+        lax.all_to_all(jnp.stack(jnp.split(local_grad, lax.axis_size("seq"), axis=0)), "seq", 0, 0),
+        axis=1,
+    )
     stretch_term = jnp.transpose(lag_acc[:, block_rows : block_rows + length]) * taps_scale
     lag_parts = lax.all_to_all(
         stretch_term.reshape(seq_count, block_rows, stretch_filters),

time: 99.2 us -> 105 us (1.058)
  local copies, waits for them, and re-layouts: 25.7 us -> 30.9 us
  waiting for transfers between devices: 43.2 us -> 44.7 us
    unnamed x17 -> x24, local copies, waits for them, and re-layouts: 5.54 us -> 10.1 us
    all_to_all x1 -> x0, other arithmetic: 2.14 us -> none  [per_device(): lax.all_to_all(local_grad, 'seq', split_axis=0, concat_axis=1, tiled=True)]
    all_to_all x1, waiting for transfers between devices: 4.37 us -> 5.87 us  [per_device(): lax.all_to_all(stretch_term.reshape(seq_count, block_rows, stretch_filter...]
    convert_element_type x0 -> x1, other arithmetic: none -> 1.32 us  [per_device(): (conv_grad + stretch_gain[None, :] * moved_grad.astype(jnp.float32)).asty...]
  transfers between devices with their start and end apart: 3 -> 3, of which waited for: 3 -> 3; matrix products, arithmetic and copies ran while one was open for 3% -> 1% of each run, Pallas kernels for 0% -> 0%
where the time goes in v1:
time: 105 us
  waiting for transfers between devices  44.7 us (43%)
  local copies, waits for them, and re-layouts  30.9 us (29%)
  starting transfers between devices  14.4 us (14%)
  matrix products  8.83 us (8%)
  other arithmetic  4.66 us (4%)
    all_to_all x1, waiting for transfers between devices, per_device(): lax.all_to_all(packed, 'seq', split_axis=1, concat_axis=0, tiled=True)  25.4 us
    all_to_all x1, waiting for transfers between devices, per_device(): lax.all_to_all(jnp.stack(jnp.split(local_grad, lax.axis_size('seq'), axis...  13.4 us
    unnamed x24, local copies, waits for them, and re-layouts  10.1 us
    all_to_all x1, starting transfers between devices, per_device(): lax.all_to_all(packed, 'seq', split_axis=1, concat_axis=0, tiled=True)  7.28 us
    dot_general x2, matrix products, advance(): jnp.einsum('kfts,iktfg->isfg', toeplitz, stacked, preferred_element_type=...  6.6 us
    all_to_all x1, waiting for transfers between devices, per_device(): lax.all_to_all(stretch_term.reshape(seq_count, block_rows, stretch_filter...  5.87 us
    reshape x2, local copies, waits for them, and re-layouts, diagonal_sums(): trimmed.reshape(products.shape[0], products.shape[1], block_rows, 2 * blo...  5.62 us
    all_to_all x1, starting transfers between devices, per_device(): lax.all_to_all(stretch_term.reshape(seq_count, block_rows, stretch_filter...  3.59 us
  transfers between devices with their start and end apart: 3, of which 3 were waited for; matrix products, arithmetic and copies ran while one was open for 1% of the time, Pallas kernels for 0%

profile of v1, /device:TPU:0, one launch (start us, length us, event | category | flops | bytes accessed | tf_op | source)
XLA Modules:
  0.0 104.5 jit_solution(15542149275491190775)
XLA Ops:
  0.7 1.4 %copy.32 = bf16[128,2048]{0,1:T(8,128)(2,1)S(1)} copy(bf16[128,2048]{1,0:T(8,128)(2,1)} %param.9) | data formatting | bytes 1048576 | tf_op args[0]
  3.1 1.1 %pad_maximum_fusion.4 = bf16[128,8,514]{0,2,1:T(8,128)(2,1)} fusion(bf16[128,8,2]{0,2,1:T(2,128)(2,1)S(1)} %bitcast.162, bf16[128,8,256]{0,2,1:T(8,128)(2,1)S(1)} %bitcast.160, bf16[128,8,256]{0,2,1:T(8,128)(2,1)S(1)} %bitcast.161), kind=kLoop, calls=%fused_computation.25 | loop fusion | flops 3158016 | bytes 2105344 | tf_op jit(solution)/shard_map/concatenate | solution.py:113
  4.2 7.3 %all-to-all-start = ((bf16[128,8,514]{0,2,1:T(8,128)(2,1)}), bf16[128,8,514]{0,2,1:T(8,128)(2,1)S(1)}, u32[]{:S(2)}, u32[]{:S(2)}) async-start(bf16[128,8,514]{0,2,1:T(8,128)(2,1)} %pad_maximum_fusion.4), calls=%async_computation | async-start | bytes 2129920 | tf_op jit(solution)/shard_map/all_to_all | solution.py:121
  11.4 0.8 dynamic_slice.63
  12.2 25.4 %all-to-all-done = bf16[128,8,514]{0,2,1:T(8,128)(2,1)S(1)} async-done(((bf16[128,8,514]{0,2,1:T(8,128)(2,1)}), bf16[128,8,514]{0,2,1:T(8,128)(2,1)S(1)}, u32[]{:S(2)}, u32[]{:S(2)}) %all-to-all-start) | async-done | bytes 1052704 | tf_op jit(solution)/shard_map/all_to_all | solution.py:121
  38.3 0.8 copy-done.3
  39.5 1.1 %copy.35 = bf16[8,128,2,128]{3,1,0,2:T(8,128)(2,1)} copy(bf16[8,128,2,128]{1,0,3,2:T(8,128)(2,1)S(1)} %bitcast.159) | data formatting | bytes 1048576
  40.6 26.8 %while.18 = (s32[]{:T(128)}, f32[8,128,2,128]{1,3,0,2:T(8,128)}, f32[2,1664]{1,0:T(2,128)S(1)}, bf16[19,128,2,128]{1,3,0,2:T(8,128)(2,1)S(1)}, bf16[2,1664]{1,0:...) while((s32[]{:T(128)}, f32[8,128,2,128]{1,3,0,2:T(8,128)}, ...), condition=%wide.region_2.3_spmd.clone, body=%wide.region_0.2_spmd.clone.sunk | while | flops 543954432 | bytes 31783416 | solution.py:86
  40.6 1.2 %dynamic-slice_bitcast_fusion.5 = (bf16[8,1,128,2,128]{2,4,1,0,3:T(8,128)(2,1)S(1)}, bf16[8,1,128,2,128]{2,4,1,0,3:T(8,128)(2,1)S(1)}, bf16[8,1,128,2,128]{2,4,1,0,3:T(8,128)(2,1)}, bf16[8,1,128,2,128]{2,4,1,0,3:T(8,128)(2,1)}) fusion(bf16[19,128,2,128]{1,3,0,2:T(8,128)(2,1)S(1)} %get-tuple-element.326, s32[]{:T(128)S(6)} %select_n.70, ...), kind=kLoop, calls=%fused_computation.9.clone.1 | loop fusion | bytes 4194320 | tf_op jit(solution)/shard_map/while/body/eval_jaxpr/stack | solution.py:49
  42.6 1.6 %reshape.112 = bf16[4,2,128,255]{3,2,1,0:T(8,128)(2,1)S(1)} reshape(bf16[4,2,32640]{2,1,0:T(2,128)(2,1)S(1)} %slice.143) | data formatting | bytes 1044480 | tf_op jit(solution)/shard_map/while/body/eval_jaxpr/reshape | solution.py:15
  44.2 3.1 %fusion.27 = f32[8,128,2,128]{1,3,0,2:T(8,128)} fusion(f32[8,128,2,128]{1,3,0,2:T(8,128)} %get-tuple-element.303, pred[]{:T(512)S(6)} %compare.9, bf16[8,1,128,2,128]{2,4,1,0,3:T(8,128)(2,1)S(1)} %get-tuple-element.271, bf16[8,1,128,2,128]{2,4,1,0,3:T(8,128)(2,1)} %get-tuple-element.272, bf16[8,1,128,2,128]{2,4,1,0,3:T(8,128)(2,1)} %get-tuple-element.273, ...), kind=kOutput, calls=%fused_computation.3.clone.1 | convolution fusion | flops 272105472 | bytes 4456449 | tf_op jit(solution)/shard_map/while/body/eval_jaxpr/kfts,iktfg->isfg/dot_general | solution.py:67
  47.3 1.1 %convolution_bitcast_fusion.3 = f32[4,2,128,128]{3,2,0,1:T(8,128)S(1)} fusion(bf16[8,128,2,128]{3,1,0,2:T(8,128)(2,1)S(1)} %copy-done.6, bf16[8,1,128,2,128]{2,4,1,0,3:T(8,128)(2,1)S(1)} %get-tuple-element.271, bf16[8,1,128,2,128]{2,4,1,0,3:T(8,128)(2,1)S(1)} %copy-done.1, bf16[8,1,128,2,128]{2,4,1,0,3:T(8,128)(2,1)S(1)} %copy-done.2, ...), kind=kOutput, calls=%fused_computation.4.clone.1 | convolution fusion | flops 271581184 | bytes 3145728 | tf_op jit(solution)/shard_map/while/body/eval_jaxpr/iktfg,isfg->kfts/dot_general | solution.py:70
  48.4 0.7 rev.25
  49.8 1.0 slice.144
  50.8 2.8 %reshape.114 = f32[4,2,128,255]{3,2,0,1:T(8,128)S(1)} reshape(f32[4,2,32640]{2,0,1:T(4,128)} %slice.144) | data formatting | bytes 2088960 | tf_op jit(solution)/shard_map/while/body/eval_jaxpr/reshape | solution.py:24
  53.9 1.2 %dynamic-slice_bitcast_fusion.5 = (bf16[8,1,128,2,128]{2,4,1,0,3:T(8,128)(2,1)S(1)}, bf16[8,1,128,2,128]{2,4,1,0,3:T(8,128)(2,1)S(1)}, bf16[8,1,128,2,128]{2,4,1,0,3:T(8,128)(2,1)}, bf16[8,1,128,2,128]{2,4,1,0,3:T(8,128)(2,1)}) fusion(bf16[19,128,2,128]{1,3,0,2:T(8,128)(2,1)S(1)} %get-tuple-element.326, s32[]{:T(128)S(6)} %select_n.70, ...), kind=kLoop, calls=%fused_computation.9.clone.1 | loop fusion | bytes 4194320 | tf_op jit(solution)/shard_map/while/body/eval_jaxpr/stack | solution.py:49
  55.8 1.6 %reshape.112 = bf16[4,2,128,255]{3,2,1,0:T(8,128)(2,1)S(1)} reshape(bf16[4,2,32640]{2,1,0:T(2,128)(2,1)S(1)} %slice.143) | data formatting | bytes 1044480 | tf_op jit(solution)/shard_map/while/body/eval_jaxpr/reshape | solution.py:15
  57.4 3.5 %fusion.27 = f32[8,128,2,128]{1,3,0,2:T(8,128)} fusion(f32[8,128,2,128]{1,3,0,2:T(8,128)} %get-tuple-element.303, pred[]{:T(512)S(6)} %compare.9, bf16[8,1,128,2,128]{2,4,1,0,3:T(8,128)(2,1)S(1)} %get-tuple-element.271, bf16[8,1,128,2,128]{2,4,1,0,3:T(8,128)(2,1)} %get-tuple-element.272, bf16[8,1,128,2,128]{2,4,1,0,3:T(8,128)(2,1)} %get-tuple-element.273, ...), kind=kOutput, calls=%fused_computation.3.clone.1 | convolution fusion | flops 272105472 | bytes 4456449 | tf_op jit(solution)/shard_map/while/body/eval_jaxpr/kfts,iktfg->isfg/dot_general | solution.py:67
  60.9 1.1 %convolution_bitcast_fusion.3 = f32[4,2,128,128]{3,2,0,1:T(8,128)S(1)} fusion(bf16[8,128,2,128]{3,1,0,2:T(8,128)(2,1)S(1)} %copy-done.6, bf16[8,1,128,2,128]{2,4,1,0,3:T(8,128)(2,1)S(1)} %get-tuple-element.271, bf16[8,1,128,2,128]{2,4,1,0,3:T(8,128)(2,1)S(1)} %copy-done.1, bf16[8,1,128,2,128]{2,4,1,0,3:T(8,128)(2,1)S(1)} %copy-done.2, ...), kind=kOutput, calls=%fused_computation.4.clone.1 | convolution fusion | flops 271581184 | bytes 3145728 | tf_op jit(solution)/shard_map/while/body/eval_jaxpr/iktfg,isfg->kfts/dot_general | solution.py:70
  62.0 0.7 rev.25
  63.4 1.0 slice.144
  64.4 2.8 %reshape.114 = f32[4,2,128,255]{3,2,0,1:T(8,128)S(1)} reshape(f32[4,2,32640]{2,0,1:T(4,128)} %slice.144) | data formatting | bytes 2088960 | tf_op jit(solution)/shard_map/while/body/eval_jaxpr/reshape | solution.py:24
  67.5 1.3 %broadcast_multiply_fusion = f32[8,128,2,128]{1,3,0,2:T(8,128)S(1)} fusion(f32[8,128,2,128]{1,3,0,2:T(8,128)} %get-tuple-element.161), kind=kLoop, calls=%fused_computation.31 | loop fusion | flops 262144 | bytes 2097152 | tf_op jit(solution)/shard_map/mul | solution.py:141
  69.4 1.3 %fusion.9 = bf16[1024,256]{0,1:T(8,128)(2,1)S(1)} fusion(f32[32,8,8,128]{3,2,1,0:T(8,128)S(1)} %bitcast.156, f32[256]{0:T(256)S(1)} %dynamic_slice.63, bf16[1024,514]{0,1:T(8,128)(2,1)} %bitcast.152), kind=kLoop, calls=%fused_computation.28 | loop fusion | flops 1048576 | bytes 2098176 | tf_op jit(solution)/shard_map/convert_element_type | solution.py:142
  70.7 0.6 fusion.17
  72.0 0.6 fusion.15
  72.7 0.6 fusion.14
  75.9 3.6 %all-to-all-start.2 = ((f32[8,128,2]{1,2,0:T(2,128)}), f32[8,128,2]{1,2,0:T(2,128)S(1)}, u32[]{:S(2)}, u32[]{:S(2)}) async-start(f32[8,128,2]{1,2,0:T(2,128)} %multiply_bitcast_fusion), calls=%async_computation.2 | async-start | bytes 16384 | tf_op jit(solution)/shard_map/all_to_all | solution.py:150
  80.1 5.9 %all-to-all-done.2 = f32[8,128,2]{1,2,0:T(2,128)S(1)} async-done(((f32[8,128,2]{1,2,0:T(2,128)}), f32[8,128,2]{1,2,0:T(2,128)S(1)}, u32[]{:S(2)}, u32[]{:S(2)}) %all-to-all-start.2) | async-done | bytes 8224 | tf_op jit(solution)/shard_map/all_to_all | solution.py:150
  86.0 3.5 %all-to-all-start.1 = ((bf16[8,128,256]{1,2,0:T(8,128)(2,1)}), bf16[8,128,256]{1,2,0:T(8,128)(2,1)S(1)}, u32[]{:S(2)}, u32[]{:S(2)}) async-start(bf16[8,128,256]{1,2,0:T(8,128)(2,1)} %fusion.10), calls=%async_computation.1 | async-start | bytes 1048576 | tf_op jit(solution)/shard_map/all_to_all | solution.py:146
  89.5 13.4 %all-to-all-done.1 = bf16[8,128,256]{1,2,0:T(8,128)(2,1)S(1)} async-done(((bf16[8,128,256]{1,2,0:T(8,128)(2,1)}), bf16[8,128,256]{1,2,0:T(8,128)(2,1)S(1)}, u32[]{:S(2)}, u32[]{:S(2)}) %all-to-all-start.1) | async-done | bytes 524320 | tf_op jit(solution)/shard_map/all_to_all | solution.py:146
  102.9 1.0 copy.38
  (68 shorter events, 10.3 us)
Async XLA Ops:
  0.6 1.9 %copy-start = (bf16[128,16]{0,1:T(8,128)(2,1)S(1)}, bf16[128,16]{0,1:T(8,128)(2,1)}, u32[]{:S(2)}) copy-start(bf16[128,16]{0,1:T(8,128)(2,1)} %param.12) | copy-start | bytes 12292
  0.6 1.4 %copy-start.4 = (bf16[128,2048]{1,0:T(8,128)(2,1)S(1)}, bf16[128,2048]{1,0:T(8,128)(2,1)}, u32[]{:S(2)}) copy-start(bf16[128,2048]{1,0:T(8,128)(2,1)} %param.10) | copy-start | bytes 1572868
  0.7 1.4 %copy-start.5 = (bf16[128,2048]{1,0:T(8,128)(2,1)S(1)}, bf16[128,2048]{1,0:T(8,128)(2,1)}, u32[]{:S(2)}) copy-start(bf16[128,2048]{1,0:T(8,128)(2,1)} %param.11) | copy-start | bytes 1572868
  4.2 33.4 %all-to-all-start = ((bf16[128,8,514]{0,2,1:T(8,128)(2,1)}), bf16[128,8,514]{0,2,1:T(8,128)(2,1)S(1)}, u32[]{:S(2)}, u32[]{:S(2)}) async-start(bf16[128,8,514]{0,2,1:T(8,128)(2,1)} %pad_maximum_fusion.4), calls=%async_computation | async-start | bytes 2129920 | tf_op jit(solution)/shard_map/all_to_all | solution.py:121
  38.1 1.0 copy-start.3
  44.1 3.2 %copy-start.1 = (bf16[8,1,128,2,128]{2,4,1,0,3:T(8,128)(2,1)S(1)}, bf16[8,1,128,2,128]{2,4,1,0,3:T(8,128)(2,1)}, u32[]{:S(2)}) copy-start(bf16[8,1,128,2,128]{2,4,1,0,3:T(8,128)(2,1)} %get-tuple-element.272) | copy-start | bytes 1572868 | tf_op jit(solution)/shard_map/while
  44.1 3.2 %copy-start.2 = (bf16[8,1,128,2,128]{2,4,1,0,3:T(8,128)(2,1)S(1)}, bf16[8,1,128,2,128]{2,4,1,0,3:T(8,128)(2,1)}, u32[]{:S(2)}) copy-start(bf16[8,1,128,2,128]{2,4,1,0,3:T(8,128)(2,1)} %get-tuple-element.273) | copy-start | bytes 1572868 | tf_op jit(solution)/shard_map/while
  44.2 3.1 %copy-start.6 = (bf16[8,128,2,128]{3,1,0,2:T(8,128)(2,1)S(1)}, bf16[8,128,2,128]{3,1,0,2:T(8,128)(2,1)}, u32[]{:S(2)}) copy-start(bf16[8,128,2,128]{3,1,0,2:T(8,128)(2,1)} %get-tuple-element.328) | copy-start | bytes 1572868 | tf_op jit(solution)/shard_map/while
  57.4 3.5 %copy-start.1 = (bf16[8,1,128,2,128]{2,4,1,0,3:T(8,128)(2,1)S(1)}, bf16[8,1,128,2,128]{2,4,1,0,3:T(8,128)(2,1)}, u32[]{:S(2)}) copy-start(bf16[8,1,128,2,128]{2,4,1,0,3:T(8,128)(2,1)} %get-tuple-element.272) | copy-start | bytes 1572868 | tf_op jit(solution)/shard_map/while
  57.4 3.5 %copy-start.2 = (bf16[8,1,128,2,128]{2,4,1,0,3:T(8,128)(2,1)S(1)}, bf16[8,1,128,2,128]{2,4,1,0,3:T(8,128)(2,1)}, u32[]{:S(2)}) copy-start(bf16[8,1,128,2,128]{2,4,1,0,3:T(8,128)(2,1)} %get-tuple-element.273) | copy-start | bytes 1572868 | tf_op jit(solution)/shard_map/while
  57.4 3.5 %copy-start.6 = (bf16[8,128,2,128]{3,1,0,2:T(8,128)(2,1)S(1)}, bf16[8,128,2,128]{3,1,0,2:T(8,128)(2,1)}, u32[]{:S(2)}) copy-start(bf16[8,128,2,128]{3,1,0,2:T(8,128)(2,1)} %get-tuple-element.328) | copy-start | bytes 1572868 | tf_op jit(solution)/shard_map/while
  75.9 10.1 %all-to-all-start.2 = ((f32[8,128,2]{1,2,0:T(2,128)}), f32[8,128,2]{1,2,0:T(2,128)S(1)}, u32[]{:S(2)}, u32[]{:S(2)}) async-start(f32[8,128,2]{1,2,0:T(2,128)} %multiply_bitcast_fusion), calls=%async_computation.2 | async-start | bytes 16384 | tf_op jit(solution)/shard_map/all_to_all | solution.py:150
  86.0 16.9 %all-to-all-start.1 = ((bf16[8,128,256]{1,2,0:T(8,128)(2,1)}), bf16[8,128,256]{1,2,0:T(8,128)(2,1)S(1)}, u32[]{:S(2)}, u32[]{:S(2)}) async-start(bf16[8,128,256]{1,2,0:T(8,128)(2,1)} %fusion.10), calls=%async_computation.1 | async-start | bytes 1048576 | tf_op jit(solution)/shard_map/all_to_all | solution.py:146
